TPU v7x, 128 devices: a whole 4x4x4 slice. The times are simulated.
128 devices in a mesh: tok: 16 (over x, y), wid: 8 (over z, core).
Axes of the slice: x: 4, y: 4, z: 4, core: 2. Of those that a mesh axis runs over, the one named last changes fastest.
Arguments:
- patches: bfloat16 [1536, 8, 6144], P('tok', None, 'wid'), may hold values from -6 to 6
- w_query: bfloat16 [6144, 4096], P('tok', 'wid'), may hold values from -0.102062073 to 0.102062073
- w_key: bfloat16 [6144, 4096], P('tok', 'wid'), may hold values from -0.102062073 to 0.102062073
- w_value: bfloat16 [6144, 4096], P('tok', 'wid'), may hold values from -0.078125 to 0.078125
- q_gain: float32 [4096], P('wid'), may hold values from 0.5 to 6
- k_gain: float32 [4096], P('wid'), may hold values from 0.5 to 6
- w_out: bfloat16 [4096, 6144], P('tok', 'wid'), may hold values from -0.09375 to 0.09375
Outputs:
- layer_out: bfloat16 [1536, 8, 6144], P('tok', None, 'wid')
All inputs are finite; a program needn't handle non-finite values.
Results may differ from a plain program's by a relative error of at most 0.0034.
The roundings to bfloat16 on the way count: a program that leaves them out, or rounds other values in their place, can miss the bound.
Values may be sent and summed in bfloat16 or wider, within the bound.
No kernel may reach another device: no remote copies, remote signals or barrier semaphores. Data moves between devices by JAX's collectives and lax.ppermute only.
A program may use at most 128 MiB of HBM per device.

v0:
```python
import jax
import jax.numpy as jnp
from jax import lax
from jax.sharding import PartitionSpec as P

D = 6144
HEAD_DIM = 128
HD = 4096


def layer_norm_rows(values, eps):
    mean = jnp.mean(values, axis=-1, keepdims=True)
    var = jnp.mean(values * values, axis=-1, keepdims=True) - mean * mean
    return (values - mean) * lax.rsqrt(var + eps)


def add_rows(left, piece):
    return jnp.dot(left, piece, preferred_element_type=jnp.float32)


def head_norm(values, gain, eps):
    rows, images, width = values.shape
    heads_here = width // HEAD_DIM
    shaped = values.reshape(rows, images, heads_here, HEAD_DIM)
    normed = layer_norm_rows(shaped, eps) * gain.reshape(heads_here, HEAD_DIM)
    return normed.astype(jnp.bfloat16).reshape(rows, images * heads_here, HEAD_DIM)


def local(patches, w_query, w_key, w_value, q_gain, k_gain, w_out):
    local_rows, images, local_width = patches.shape
    as_float = patches.astype(jnp.float32)
    totals = lax.psum((jnp.sum(as_float, axis=-1), jnp.sum(as_float * as_float, axis=-1)), "wid")
    mean = totals[0] / D
    var = totals[1] / D - mean * mean
    normed = ((as_float - mean[..., None]) * lax.rsqrt(var + 1e-06)[..., None]).astype(jnp.bfloat16)
    whole = lax.all_gather(normed, "wid", axis=2, tiled=True)
    flat = whole.reshape(local_rows * images, D)

    def add_one(piece):
        return add_rows(flat, piece)

    query = add_one(lax.all_gather(w_query, "tok", axis=0, tiled=True))
    key = add_one(lax.all_gather(w_key, "tok", axis=0, tiled=True))
    value = add_one(lax.all_gather(w_value, "tok", axis=0, tiled=True))
    head_width = query.shape[1]
    heads_here = head_width // HEAD_DIM
    qnorm = head_norm(query.reshape(local_rows, images, head_width), q_gain, 1e-06)
    knorm = head_norm(key.reshape(local_rows, images, head_width), k_gain, 1e-06)
    vshaped = value.astype(jnp.bfloat16).reshape(local_rows, images * heads_here, HEAD_DIM)
    qfull, kfull, vfull = (
        lax.all_to_all(qnorm, "tok", split_axis=1, concat_axis=0, tiled=True),
        lax.all_to_all(knorm, "tok", split_axis=1, concat_axis=0, tiled=True),
        lax.all_to_all(vshaped, "tok", split_axis=1, concat_axis=0, tiled=True),
    )
    seq_rows, item_count, _ = qfull.shape
    block = min(512, seq_rows)
    blocks = qfull.reshape(seq_rows // block, block, item_count, HEAD_DIM)
    scale = HEAD_DIM ** (-0.5)

    def attend(qblock):
        scores = (
            jnp.einsum("qid,kid->iqk", qblock, kfull, preferred_element_type=jnp.float32) * scale
        )
        top = jnp.max(scores, axis=-1, keepdims=True)
        expo = jnp.exp(scores - top)
        probs = (expo / jnp.sum(expo, axis=-1, keepdims=True)).astype(jnp.bfloat16)
        return jnp.einsum("iqk,kid->qid", probs, vfull, preferred_element_type=jnp.float32).astype(
            jnp.bfloat16
        )

    attended = lax.map(attend, blocks).reshape(seq_rows, item_count, HEAD_DIM)
    returned = lax.all_to_all(attended, "tok", split_axis=0, concat_axis=1, tiled=True)
    mixed = returned.reshape(local_rows, images, head_width)
    mixed_whole = lax.all_gather(mixed, "wid", axis=2, tiled=True).reshape(local_rows * images, HD)
    branch = add_rows(mixed_whole, lax.all_gather(w_out, "tok", axis=0, tiled=True))
    return (as_float + branch.reshape(local_rows, images, local_width)).astype(jnp.bfloat16)


def solution(mesh):
    placed = (
        P("tok", None, "wid"),
        P("tok", "wid"),
        P("tok", "wid"),
        P("tok", "wid"),
        P("wid"),
        P("wid"),
        P("tok", "wid"),
    )
    return jax.shard_map(
        local, mesh=mesh, in_specs=placed, out_specs=P("tok", None, "wid"), check_vma=False
    )
```

profile of v0, /device:TPU:1, one launch (start us, length us, event | category | flops | bytes accessed | tf_op | source)
XLA Modules:
  0.0 413.2 jit_solution(13096195138960030265)
XLA Ops:
  8.1 1.8 convert_reduce_fusion
  9.9 14.7 %all-reduce = (f32[96,8]{0,1:T(8,128)S(1)}, f32[96,8]{0,1:T(8,128)S(1)}) all-reduce(f32[96,8]{0,1:T(8,128)S(1)} %copy.64, f32[96,8]{0,1:T(8,128)S(1)} %copy.62), channel_id=1, replica_groups=mesh['tok'=16,'wid'=8] {'wid'}, use_global_device_ids=true, to_apply=%region_3.0 | all-reduce | flops 1536 | bytes 12288 | tf_op jit(solution)/shard_map/psum | solution.py:32
  24.8 2.6 fusion.36
  28.6 45.1 %all-gather.11.cloned.1.call-done = bf16[6144,512]{1,0:T(8,128)(2,1)} async-done(((bf16[384,512]{1,0:T(8,128)(2,1)}), bf16[6144,512]{1,0:T(8,128)(2,1)}) %all-gather.11.cloned.1.call-update) | async-done | bytes 6291472 | tf_op jit(solution)/shard_map/all_gather | solution.py:43
  73.7 8.6 %copy.73 = bf16[512,6144]{1,0:T(8,128)(2,1)} copy(bf16[512,6144]{0,1:T(8,128)(2,1)} %bitcast.87) | data formatting | bytes 12582912 | tf_op jit(solution)/shard_map/dot_general | solution.py:18
  82.4 54.4 %all-gather.9.cloned.1.call-done = bf16[6144,512]{1,0:T(8,128)(2,1)} async-done(((bf16[384,512]{1,0:T(8,128)(2,1)}), bf16[6144,512]{1,0:T(8,128)(2,1)}) %all-gather.9.cloned.1.call-update) | async-done | bytes 6291472 | tf_op jit(solution)/shard_map/all_gather | solution.py:42
  136.8 8.7 %copy.66 = bf16[512,6144]{1,0:T(8,128)(2,1)} copy(bf16[512,6144]{0,1:T(8,128)(2,1)} %bitcast.88) | data formatting | bytes 12582912 | tf_op jit(solution)/shard_map/dot_general | solution.py:18
  145.5 47.6 %all-gather.7.cloned.1.call-done = bf16[96,8,6144]{2,1,0:T(8,128)(2,1)} async-done(((bf16[96,8,768]{2,1,0:T(8,128)(2,1)}), bf16[96,8,6144]{2,1,0:T(8,128)(2,1)}) %all-gather.7.cloned.1.call-update) | async-done | bytes 9437200 | tf_op jit(solution)/shard_map/all_gather | solution.py:36
  193.1 9.8 %fusion.44 = (f32[96,8,4]{1,2,0:T(4,128)S(1)}, f32[96,8,4]{1,2,0:T(4,128)S(1)}, f32[96,8,4,128]{3,1,2,0:T(8,128)S(1)}) fusion(bf16[4,128,6144,1]{2,1,0,3:T(8,128)(2,1)} %bitcast.90, bf16[96,8,6144]{2,1,0:T(8,128)(2,1)} %all-gather.7.cloned.1.call-done), kind=kOutput, calls=%fused_computation.46 | convolution fusion | flops 4833011712 | bytes 17326080 | tf_op jit(solution)/shard_map/dot_general | solution.py:18
  204.4 1.2 copy.78
  205.6 6.5 %all-to-all-start.1 = ((bf16[96,32,128]{2,0,1:T(8,128)(2,1)}), bf16[96,32,128]{2,0,1:T(8,128)(2,1)S(1)}, u32[]{:S(2)}, u32[]{:S(2)}) async-start(bf16[96,32,128]{2,0,1:T(8,128)(2,1)} %bitcast.18), calls=%async_computation.1 | async-start | bytes 1572864 | tf_op jit(solution)/shard_map/all_to_all | solution.py:52
  212.1 9.8 %fusion.45 = (f32[96,8,4]{1,2,0:T(4,128)S(1)}, f32[96,8,4]{1,2,0:T(4,128)S(1)}, f32[96,8,4,128]{3,1,2,0:T(8,128)S(1)}) fusion(bf16[4,128,6144,1]{2,1,0,3:T(8,128)(2,1)} %bitcast.89, bf16[96,8,6144]{2,1,0:T(8,128)(2,1)} %all-gather.7.cloned.1.call-done), kind=kOutput, calls=%fused_computation.47 | convolution fusion | flops 4833011712 | bytes 17326080 | tf_op jit(solution)/shard_map/dot_general | solution.py:18
  223.4 1.2 copy.71
  224.6 2.4 all-to-all-done.1
  227.0 4.2 %all-to-all-start = ((bf16[96,32,128]{2,0,1:T(8,128)(2,1)}), bf16[96,32,128]{2,0,1:T(8,128)(2,1)S(1)}, u32[]{:S(2)}, u32[]{:S(2)}) async-start(bf16[96,32,128]{2,0,1:T(8,128)(2,1)} %bitcast.9), calls=%async_computation | async-start | bytes 1572864 | tf_op jit(solution)/shard_map/all_to_all | solution.py:51
  231.3 38.9 %all-gather.13.cloned.1.call-done = bf16[6144,512]{1,0:T(8,128)(2,1)} async-done(((bf16[384,512]{1,0:T(8,128)(2,1)}), bf16[6144,512]{1,0:T(8,128)(2,1)}) %all-gather.13.cloned.1.call-update) | async-done | bytes 6291472 | tf_op jit(solution)/shard_map/all_gather | solution.py:44
  270.2 9.9 %fusion.41 = bf16[768,512]{1,0:T(8,128)(2,1)S(1)} fusion(bf16[6144,512]{1,0:T(8,128)(2,1)} %all-gather.13.cloned.1.call-done, bf16[96,8,6144]{2,1,0:T(8,128)(2,1)} %all-gather.7.cloned.1.call-done), kind=kOutput, calls=%fused_computation.39 | convolution fusion | flops 4832231424 | bytes 16515072 | tf_op jit(solution)/shard_map/dot_general | solution.py:18
  280.6 1.2 copy.80
  281.8 4.3 %all-to-all-start.2 = ((bf16[96,32,128]{2,0,1:T(8,128)(2,1)}), bf16[96,32,128]{2,0,1:T(8,128)(2,1)S(1)}, u32[]{:S(2)}, u32[]{:S(2)}) async-start(bf16[96,32,128]{2,0,1:T(8,128)(2,1)} %copy.80), calls=%async_computation.2 | async-start | bytes 1572864 | tf_op jit(solution)/shard_map/all_to_all | solution.py:53
  286.2 14.3 %all-to-all-done.2 = bf16[96,32,128]{2,0,1:T(8,128)(2,1)S(1)} async-done(((bf16[96,32,128]{2,0,1:T(8,128)(2,1)}), bf16[96,32,128]{2,0,1:T(8,128)(2,1)S(1)}, u32[]{:S(2)}, u32[]{:S(2)}) %all-to-all-start.2) | async-done | bytes 786464 | tf_op jit(solution)/shard_map/all_to_all | solution.py:53
  300.6 27.7 %while.10 = (s32[]{:T(128)}, bf16[3,512,2,128]{3,1,0,2:T(8,128)(2,1)}, bf16[3,512,2,128]{3,1,0,2:T(8,128)(2,1)S(1)}, bf16[1536,2,128]{2,0,1:T(8,128)(2,1)S(1)}, bf16[1536,2,128]{2,0,1:T(8,128)(2,1)S(1)}, /*index=5*/s32[]{:T(128)}) while((s32[]{:T(128)}, bf16[3,512,2,128]{3,1,0,2:T(8,128)(2,1)}, bf16[3,512,2,128]{3,1,0,2:T(8,128)(2,1)S(1)}, ...), condition=%wide.region_11.12_spmd, body=%wide.region_8.11_spmd.sunk | while | flops 813303296 | bytes 14688841 | solution.py:71
  300.6 4.6 %fusion.66 = (f32[2,512]{1,0:T(2,128)S(1)}, f32[2,512,1536]{2,1,0:T(8,128)}) fusion(bf16[1536,2,128]{2,0,1:T(8,128)(2,1)S(1)} %get-tuple-element.136, bf16[3,512,2,128]{3,1,0,2:T(8,128)(2,1)S(1)} %get-tuple-element.135, s32[]{:T(128)} %get-tuple-element.127), kind=kOutput, calls=%fused_computation.48.clone.1 | convolution fusion | flops 407373312 | bytes 7344132 | tf_op jit(solution)/shard_map/while/body/eval_jaxpr/sub | solution.py:65
  305.2 4.5 %fusion.67 = bf16[3,512,2,128]{3,1,0,2:T(8,128)(2,1)} fusion(bf16[3,512,2,128]{3,1,0,2:T(8,128)(2,1)} %get-tuple-element.128, s32[]{:T(128)} %get-tuple-element.127, bf16[1536,2,128]{2,0,1:T(8,128)(2,1)S(1)} %get-tuple-element.137, f32[2,512,1536]{2,1,0:T(8,128)} %get-tuple-element.119, f32[2,512]{1,0:T(2,128)S(1)} %get-tuple-element.120), kind=kOutput, calls=%fused_computation.9.clone.1 | convolution fusion | flops 405929984 | bytes 7344640 | tf_op jit(solution)/shard_map/while/body/eval_jaxpr/iqk,kid->qid/dot_general | solution.py:67
  309.7 4.6 %fusion.66 = (f32[2,512]{1,0:T(2,128)S(1)}, f32[2,512,1536]{2,1,0:T(8,128)}) fusion(bf16[1536,2,128]{2,0,1:T(8,128)(2,1)S(1)} %get-tuple-element.136, bf16[3,512,2,128]{3,1,0,2:T(8,128)(2,1)S(1)} %get-tuple-element.135, s32[]{:T(128)} %get-tuple-element.127), kind=kOutput, calls=%fused_computation.48.clone.1 | convolution fusion | flops 407373312 | bytes 7344132 | tf_op jit(solution)/shard_map/while/body/eval_jaxpr/sub | solution.py:65
  314.4 4.6 %fusion.67 = bf16[3,512,2,128]{3,1,0,2:T(8,128)(2,1)} fusion(bf16[3,512,2,128]{3,1,0,2:T(8,128)(2,1)} %get-tuple-element.128, s32[]{:T(128)} %get-tuple-element.127, bf16[1536,2,128]{2,0,1:T(8,128)(2,1)S(1)} %get-tuple-element.137, f32[2,512,1536]{2,1,0:T(8,128)} %get-tuple-element.119, f32[2,512]{1,0:T(2,128)S(1)} %get-tuple-element.120), kind=kOutput, calls=%fused_computation.9.clone.1 | convolution fusion | flops 405929984 | bytes 7344640 | tf_op jit(solution)/shard_map/while/body/eval_jaxpr/iqk,kid->qid/dot_general | solution.py:67
  319.0 4.6 %fusion.66 = (f32[2,512]{1,0:T(2,128)S(1)}, f32[2,512,1536]{2,1,0:T(8,128)}) fusion(bf16[1536,2,128]{2,0,1:T(8,128)(2,1)S(1)} %get-tuple-element.136, bf16[3,512,2,128]{3,1,0,2:T(8,128)(2,1)S(1)} %get-tuple-element.135, s32[]{:T(128)} %get-tuple-element.127), kind=kOutput, calls=%fused_computation.48.clone.1 | convolution fusion | flops 407373312 | bytes 7344132 | tf_op jit(solution)/shard_map/while/body/eval_jaxpr/sub | solution.py:65
  323.6 4.6 %fusion.67 = bf16[3,512,2,128]{3,1,0,2:T(8,128)(2,1)} fusion(bf16[3,512,2,128]{3,1,0,2:T(8,128)(2,1)} %get-tuple-element.128, s32[]{:T(128)} %get-tuple-element.127, bf16[1536,2,128]{2,0,1:T(8,128)(2,1)S(1)} %get-tuple-element.137, f32[2,512,1536]{2,1,0:T(8,128)} %get-tuple-element.119, f32[2,512]{1,0:T(2,128)S(1)} %get-tuple-element.120), kind=kOutput, calls=%fused_computation.9.clone.1 | convolution fusion | flops 405929984 | bytes 7344640 | tf_op jit(solution)/shard_map/while/body/eval_jaxpr/iqk,kid->qid/dot_general | solution.py:67
  328.3 6.8 %copy.84 = bf16[1536,2,128]{2,1,0:T(2,128)(2,1)S(1)} copy(bf16[1536,2,128]{2,0,1:T(8,128)(2,1)} %bitcast.98) | data formatting | bytes 1572864 | tf_op jit(solution)/shard_map/reshape | solution.py:71
  335.1 18.8 %all_to_all.66 = bf16[1536,2,128]{2,1,0:T(2,128)(2,1)S(1)} all-to-all(bf16[1536,2,128]{2,1,0:T(2,128)(2,1)S(1)} %copy.84), channel_id=1, replica_groups=mesh['tok'=16,'wid'=8] {'tok'}, dimensions={0} | all-to-all | bytes 1572864 | tf_op jit(solution)/shard_map/all_to_all | solution.py:72
  354.8 1.2 reshape.81
  356.1 40.5 %all-gather.15.cloned.1.call-done = bf16[96,8,4096]{2,1,0:T(8,128)(2,1)} async-done(((bf16[96,8,512]{2,1,0:T(8,128)(2,1)}), bf16[96,8,4096]{2,1,0:T(8,128)(2,1)}) %all-gather.15.cloned.1.call-update) | async-done | bytes 6291472 | tf_op jit(solution)/shard_map/all_gather | solution.py:74
  396.5 9.8 %fusion.38 = bf16[96,8,768]{2,1,0:T(8,128)(2,1)} fusion(bf16[96,8,768]{2,1,0:T(8,128)(2,1)S(1)} %copy-done, bf16[96,8,4096]{2,1,0:T(8,128)(2,1)} %all-gather.15.cloned.1.call-done, bf16[4096,768]{1,0:T(8,128)(2,1)} %all-gather.17.cloned.1.call-done), kind=kOutput, calls=%fused_computation.34 | convolution fusion | flops 4833607680 | bytes 14942208 | tf_op jit(solution)/shard_map/dot_general | solution.py:18
  (44 shorter events, 7.5 us)
Async XLA Ops:
  6.5 67.2 %all-gather.11.cloned.1.call-start = ((), (), s32[]{:S(2)}) async-start(), calls=%async_computation.6 | async-start | bytes 6684672 | tf_op jit(solution)/shard_map/all_gather | solution.py:43
  7.3 129.5 %all-gather.9.cloned.1.call-start = ((), (), s32[]{:S(2)}) async-start(), calls=%async_computation.5 | async-start | bytes 6684672 | tf_op jit(solution)/shard_map/all_gather | solution.py:42
  8.0 185.1 %all-gather.7.cloned.1.call-start = ((), (), s32[]{:S(2)}) async-start(), calls=%async_computation.4 | async-start | bytes 10616832 | tf_op jit(solution)/shard_map/all_gather | solution.py:36
  27.5 242.7 %all-gather.13.cloned.1.call-start = ((), (), s32[]{:S(2)}) async-start(), calls=%async_computation.7 | async-start | bytes 6684672 | tf_op jit(solution)/shard_map/all_gather | solution.py:44
  28.1 328.0 %all-gather.17.cloned.1.call-start = ((), (), s32[]{:S(2)}) async-start(), calls=%async_computation.9 | async-start | bytes 6684672 | tf_op jit(solution)/shard_map/all_gather | solution.py:75
  193.1 10.3 %copy-start.1 = (f32[512]{0:T(512)S(1)}, f32[512]{0:T(512)}, u32[]{:S(2)}) copy-start(f32[512]{0:T(512)} %param.14) | copy-start | bytes 6148
  205.6 21.5 %all-to-all-start.1 = ((bf16[96,32,128]{2,0,1:T(8,128)(2,1)}), bf16[96,32,128]{2,0,1:T(8,128)(2,1)S(1)}, u32[]{:S(2)}, u32[]{:S(2)}) async-start(bf16[96,32,128]{2,0,1:T(8,128)(2,1)} %bitcast.18), calls=%async_computation.1 | async-start | bytes 1572864 | tf_op jit(solution)/shard_map/all_to_all | solution.py:52
  212.1 10.3 %copy-start.2 = (f32[512]{0:T(512)S(1)}, f32[512]{0:T(512)}, u32[]{:S(2)}) copy-start(f32[512]{0:T(512)} %param.13) | copy-start | bytes 6148
  227.0 54.7 %all-to-all-start = ((bf16[96,32,128]{2,0,1:T(8,128)(2,1)}), bf16[96,32,128]{2,0,1:T(8,128)(2,1)S(1)}, u32[]{:S(2)}, u32[]{:S(2)}) async-start(bf16[96,32,128]{2,0,1:T(8,128)(2,1)} %bitcast.9), calls=%async_computation | async-start | bytes 1572864 | tf_op jit(solution)/shard_map/all_to_all | solution.py:51
  281.8 18.8 %all-to-all-start.2 = ((bf16[96,32,128]{2,0,1:T(8,128)(2,1)}), bf16[96,32,128]{2,0,1:T(8,128)(2,1)S(1)}, u32[]{:S(2)}, u32[]{:S(2)}) async-start(bf16[96,32,128]{2,0,1:T(8,128)(2,1)} %copy.80), calls=%async_computation.2 | async-start | bytes 1572864 | tf_op jit(solution)/shard_map/all_to_all | solution.py:53
  286.0 110.5 %all-gather.15.cloned.1.call-start = ((), (), s32[]{:S(2)}) async-start(), calls=%async_computation.8 | async-start | bytes 7077888 | tf_op jit(solution)/shard_map/all_gather | solution.py:74
  328.3 68.3 %copy-start = (bf16[96,8,768]{2,1,0:T(8,128)(2,1)S(1)}, bf16[96,8,768]{2,1,0:T(8,128)(2,1)}, u32[]{:S(2)}) copy-start(bf16[96,8,768]{2,1,0:T(8,128)(2,1)} %param.9) | copy-start | bytes 3538948
Sparse Core Ops, SparseCore 0:
  9.5 64.1 all-gather.10
  75.9 60.8 all-gather.8
  138.5 54.5 all-gather.6
  195.1 75.0 all-gather.12
  272.2 66.2 all-gather.16
  356.1 40.3 all-gather.14
where the time goes:
time: 414 us; the launch traced here: 413 us
  waiting for transfers between devices  246 us (59%)
  matrix products  66.9 us (16%)
  blocking collectives  33.5 us (8%)
  local copies, waits for them, and re-layouts  31.7 us (8%)
  starting transfers between devices  15.2 us (4%)
  between operations  13.7 us (3%)
  other arithmetic  6.42 us (2%)
    all_gather x1, waiting for transfers between devices, local(): query = add_one(lax.all_gather(w_query, 'tok', axis=0, tiled=True))  54.4 us
    all_gather x1, waiting for transfers between devices, local(): whole = lax.all_gather(normed, 'wid', axis=2, tiled=True)  47.6 us
    all_gather x1, waiting for transfers between devices, local(): key = add_one(lax.all_gather(w_key, 'tok', axis=0, tiled=True))  45.1 us
    all_gather x1, waiting for transfers between devices, local(): lax.all_gather(mixed, 'wid', axis=2, tiled=True)  40.5 us
    dot_general x4, matrix products, add_rows(): return jnp.dot(left, piece, preferred_element_type=jnp.float32)  39.2 us
    all_gather x1, waiting for transfers between devices, local(): value = add_one(lax.all_gather(w_value, 'tok', axis=0, tiled=True))  38.9 us
    all_to_all x1, blocking collectives, local(): lax.all_to_all(attended, 'tok', split_axis=0, concat_axis=1, tiled=True)  18.8 us
    dot_general x2, local copies, waits for them, and re-layouts, add_rows(): return jnp.dot(left, piece, preferred_element_type=jnp.float32)  17.4 us
  transfers between devices with their start and end apart: 9, of which 7 were waited for; matrix products, arithmetic and copies ran while one was open for 23% of the time, Pallas kernels for 0%

commit v1 on v0

--- a/solution.py
+++ b/solution.py
@@ -49,7 +49,10 @@
     vshaped = value.astype(jnp.bfloat16).reshape(local_rows, images * heads_here, HEAD_DIM)
     qfull, kfull, vfull = (
         lax.all_to_all(qnorm, "tok", split_axis=1, concat_axis=0, tiled=True),
-        lax.all_to_all(knorm, "tok", split_axis=1, concat_axis=0, tiled=True),
+        jnp.concatenate(
+            lax.all_to_all(jnp.stack(jnp.split(knorm, lax.axis_size("tok"), axis=1)), "tok", 0, 0),
+            axis=0,
+        ),
         lax.all_to_all(vshaped, "tok", split_axis=1, concat_axis=0, tiled=True),
     )
     seq_rows, item_count, _ = qfull.shape

time: 414 us -> 434 us (1.048)
  local copies, waits for them, and re-layouts: 31.7 us -> 43.2 us
  waiting for transfers between devices: 246 us -> 256 us
    all_to_all x1, waiting for transfers between devices: 2.42 us -> 18.9 us  [local(): lax.all_to_all(jnp.stack(jnp.split(knorm, lax.axis_size('tok'), axis=1)),...]
    unnamed x6 -> x21, local copies, waits for them, and re-layouts: 0.01 us -> 9.34 us
    all_gather x1, waiting for transfers between devices: 38.9 us -> 33.1 us  [local(): value = add_one(lax.all_gather(w_value, 'tok', axis=0, tiled=True))]
  transfers between devices with their start and end apart: 9 -> 9, of which waited for: 7 -> 7; matrix products, arithmetic and copies ran while one was open for 23% -> 25% of each run, Pallas kernels for 0% -> 0%
where the time goes in v1:
time: 434 us; the launch traced here: 433 us
  waiting for transfers between devices  256 us (59%)
  matrix products  64.8 us (15%)
  local copies, waits for them, and re-layouts  43.2 us (10%)
  blocking collectives  32 us (7%)
  starting transfers between devices  15.2 us (4%)
  between operations  13.7 us (3%)
  other arithmetic  8.4 us (2%)
    all_gather x1, waiting for transfers between devices, local(): query = add_one(lax.all_gather(w_query, 'tok', axis=0, tiled=True))  54.4 us
    all_gather x1, waiting for transfers between devices, local(): whole = lax.all_gather(normed, 'wid', axis=2, tiled=True)  47.6 us
    all_gather x1, waiting for transfers between devices, local(): key = add_one(lax.all_gather(w_key, 'tok', axis=0, tiled=True))  45.1 us
    all_gather x1, waiting for transfers between devices, local(): lax.all_gather(mixed, 'wid', axis=2, tiled=True)  41.2 us
    dot_general x4, matrix products, add_rows(): return jnp.dot(left, piece, preferred_element_type=jnp.float32)  37.3 us
    all_gather x1, waiting for transfers between devices, local(): value = add_one(lax.all_gather(w_value, 'tok', axis=0, tiled=True))  33.1 us
    all_to_all x1, waiting for transfers between devices, local(): lax.all_to_all(jnp.stack(jnp.split(knorm, lax.axis_size('tok'), axis=1)),...  18.9 us
    dot_general x2, local copies, waits for them, and re-layouts, add_rows(): return jnp.dot(left, piece, preferred_element_type=jnp.float32)  17.4 us
  transfers between devices with their start and end apart: 9, of which 7 were waited for; matrix products, arithmetic and copies ran while one was open for 25% of the time, Pallas kernels for 0%

profile of v1, /device:TPU:1, one launch (start us, length us, event | category | flops | bytes accessed | tf_op | source)
XLA Modules:
  0.0 432.9 jit_solution(12036060431801987641)
XLA Ops:
  8.1 1.8 convert_reduce_fusion
  9.9 14.7 %all-reduce = (f32[96,8]{0,1:T(8,128)S(1)}, f32[96,8]{0,1:T(8,128)S(1)}) all-reduce(f32[96,8]{0,1:T(8,128)S(1)} %copy.79, f32[96,8]{0,1:T(8,128)S(1)} %copy.77), channel_id=1, replica_groups=mesh['tok'=16,'wid'=8] {'wid'}, use_global_device_ids=true, to_apply=%region_3.0 | all-reduce | flops 1536 | bytes 12288 | tf_op jit(solution)/shard_map/psum | solution.py:32
  24.8 2.6 fusion.36
  28.6 45.1 %all-gather.11.cloned.1.call-done = bf16[6144,512]{1,0:T(8,128)(2,1)} async-done(((bf16[384,512]{1,0:T(8,128)(2,1)}), bf16[6144,512]{1,0:T(8,128)(2,1)}) %all-gather.11.cloned.1.call-update) | async-done | bytes 6291472 | tf_op jit(solution)/shard_map/all_gather | solution.py:43
  73.7 8.6 %copy.88 = bf16[512,6144]{1,0:T(8,128)(2,1)} copy(bf16[512,6144]{0,1:T(8,128)(2,1)} %bitcast.148) | data formatting | bytes 12582912 | tf_op jit(solution)/shard_map/dot_general | solution.py:18
  82.4 54.4 %all-gather.9.cloned.1.call-done = bf16[6144,512]{1,0:T(8,128)(2,1)} async-done(((bf16[384,512]{1,0:T(8,128)(2,1)}), bf16[6144,512]{1,0:T(8,128)(2,1)}) %all-gather.9.cloned.1.call-update) | async-done | bytes 6291472 | tf_op jit(solution)/shard_map/all_gather | solution.py:42
  136.8 8.7 %copy.81 = bf16[512,6144]{1,0:T(8,128)(2,1)} copy(bf16[512,6144]{0,1:T(8,128)(2,1)} %bitcast.149) | data formatting | bytes 12582912 | tf_op jit(solution)/shard_map/dot_general | solution.py:18
  145.5 47.6 %all-gather.7.cloned.1.call-done = bf16[96,8,6144]{2,1,0:T(8,128)(2,1)} async-done(((bf16[96,8,768]{2,1,0:T(8,128)(2,1)}), bf16[96,8,6144]{2,1,0:T(8,128)(2,1)}) %all-gather.7.cloned.1.call-update) | async-done | bytes 9437200 | tf_op jit(solution)/shard_map/all_gather | solution.py:36
  193.1 10.7 %fusion.60 = (f32[96,8,4]{1,2,0:T(4,128)S(1)}, f32[96,8,4]{1,2,0:T(4,128)S(1)}, f32[96,8,4,128]{3,1,2,0:T(8,128)S(1)}) fusion(bf16[4,128,6144,1]{2,1,0,3:T(8,128)(2,1)} %bitcast.150, bf16[96,8,6144]{2,1,0:T(8,128)(2,1)} %all-gather.7.cloned.1.call-done), kind=kOutput, calls=%fused_computation.78 | convolution fusion | flops 4833011712 | bytes 17326080 | tf_op jit(solution)/shard_map/dot_general | solution.py:18
  203.8 6.9 %fusion.61 = (f32[96,8,4]{1,2,0:T(4,128)}, f32[96,8,4]{1,2,0:T(4,128)}, f32[96,8,4,128]{3,1,2,0:T(8,128)S(1)}) fusion(bf16[4,128,6144,1]{2,1,0,3:T(8,128)(2,1)S(1)} %bitcast.151, bf16[96,8,6144]{2,1,0:T(8,128)(2,1)S(1)} %copy-done.2), kind=kOutput, calls=%fused_computation.79 | convolution fusion | flops 4833011712 | bytes 17326080 | tf_op jit(solution)/shard_map/dot_general | solution.py:18
  212.5 1.7 multiply_convert_fusion
  216.8 1.7 multiply_convert_fusion.1
  218.5 1.2 copy.86
  219.7 6.5 %all-to-all-start = ((bf16[96,32,128]{2,0,1:T(8,128)(2,1)}), bf16[96,32,128]{2,0,1:T(8,128)(2,1)S(1)}, u32[]{:S(2)}, u32[]{:S(2)}) async-start(bf16[96,32,128]{2,0,1:T(8,128)(2,1)} %bitcast.9), calls=%async_computation | async-start | bytes 1572864 | tf_op jit(solution)/shard_map/all_to_all | solution.py:51
  231.2 33.1 %all-gather.13.cloned.1.call-done = bf16[6144,512]{1,0:T(8,128)(2,1)} async-done(((bf16[384,512]{1,0:T(8,128)(2,1)}), bf16[6144,512]{1,0:T(8,128)(2,1)}) %all-gather.13.cloned.1.call-update) | async-done | bytes 6291472 | tf_op jit(solution)/shard_map/all_gather | solution.py:44
  264.3 9.9 %fusion.41 = bf16[768,512]{1,0:T(8,128)(2,1)S(1)} fusion(bf16[6144,512]{1,0:T(8,128)(2,1)} %all-gather.13.cloned.1.call-done, bf16[96,8,6144]{2,1,0:T(8,128)(2,1)} %all-gather.7.cloned.1.call-done), kind=kOutput, calls=%fused_computation.39 | convolution fusion | flops 4832231424 | bytes 16515072 | tf_op jit(solution)/shard_map/dot_general | solution.py:18
  275.3 1.2 copy.95
  278.3 4.8 %all-to-all-start.2 = ((bf16[96,32,128]{2,0,1:T(8,128)(2,1)}), bf16[96,32,128]{2,0,1:T(8,128)(2,1)S(1)}, u32[]{:S(2)}, u32[]{:S(2)}) async-start(bf16[96,32,128]{2,0,1:T(8,128)(2,1)} %copy.95), calls=%async_computation.2 | async-start | bytes 1572864 | tf_op jit(solution)/shard_map/all_to_all | solution.py:56
  285.7 12.8 %all-to-all-done.2 = bf16[96,32,128]{2,0,1:T(8,128)(2,1)S(1)} async-done(((bf16[96,32,128]{2,0,1:T(8,128)(2,1)}), bf16[96,32,128]{2,0,1:T(8,128)(2,1)S(1)}, u32[]{:S(2)}, u32[]{:S(2)}) %all-to-all-start.2) | async-done | bytes 786464 | tf_op jit(solution)/shard_map/all_to_all | solution.py:56
  298.5 3.6 all-to-all-start.1
  302.3 18.9 %all-to-all-done.1 = bf16[16,96,2,128]{3,1,2,0:T(8,128)(2,1)S(1)} async-done(((bf16[16,96,2,128]{3,1,2,0:T(8,128)(2,1)}), bf16[16,96,2,128]{3,1,2,0:T(8,128)(2,1)S(1)}, u32[]{:S(2)}, u32[]{:S(2)}) %all-to-all-start.1) | async-done | bytes 786464 | tf_op jit(solution)/shard_map/all_to_all | solution.py:53
  321.3 27.6 %while.10 = (s32[]{:T(128)}, bf16[3,512,2,128]{3,1,0,2:T(8,128)(2,1)}, bf16[3,512,2,128]{3,1,0,2:T(8,128)(2,1)S(1)}, bf16[1536,2,128]{2,0,1:T(8,128)(2,1)S(1)}, bf16[1536,2,128]{2,0,1:T(8,128)(2,1)S(1)}, /*index=5*/s32[]{:T(128)}) while((s32[]{:T(128)}, bf16[3,512,2,128]{3,1,0,2:T(8,128)(2,1)}, bf16[3,512,2,128]{3,1,0,2:T(8,128)(2,1)S(1)}, ...), condition=%wide.region_11.12_spmd, body=%wide.region_8.11_spmd.sunk | while | flops 813303296 | bytes 14688841 | solution.py:74
  321.3 4.6 %fusion.82 = (f32[2,512]{1,0:T(2,128)S(1)}, f32[2,512,1536]{2,1,0:T(8,128)}) fusion(bf16[1536,2,128]{2,0,1:T(8,128)(2,1)S(1)} %get-tuple-element.136, bf16[3,512,2,128]{3,1,0,2:T(8,128)(2,1)S(1)} %get-tuple-element.135, s32[]{:T(128)} %get-tuple-element.127), kind=kOutput, calls=%fused_computation.80.clone.1 | convolution fusion | flops 407373312 | bytes 7344132 | tf_op jit(solution)/shard_map/while/body/eval_jaxpr/sub | solution.py:68
  325.9 4.6 %fusion.83 = bf16[3,512,2,128]{3,1,0,2:T(8,128)(2,1)} fusion(bf16[3,512,2,128]{3,1,0,2:T(8,128)(2,1)} %get-tuple-element.128, s32[]{:T(128)} %get-tuple-element.127, bf16[1536,2,128]{2,0,1:T(8,128)(2,1)S(1)} %get-tuple-element.137, f32[2,512,1536]{2,1,0:T(8,128)} %get-tuple-element.119, f32[2,512]{1,0:T(2,128)S(1)} %get-tuple-element.120), kind=kOutput, calls=%fused_computation.9.clone.1 | convolution fusion | flops 405929984 | bytes 7344640 | tf_op jit(solution)/shard_map/while/body/eval_jaxpr/iqk,kid->qid/dot_general | solution.py:70
  330.6 4.6 %fusion.82 = (f32[2,512]{1,0:T(2,128)S(1)}, f32[2,512,1536]{2,1,0:T(8,128)}) fusion(bf16[1536,2,128]{2,0,1:T(8,128)(2,1)S(1)} %get-tuple-element.136, bf16[3,512,2,128]{3,1,0,2:T(8,128)(2,1)S(1)} %get-tuple-element.135, s32[]{:T(128)} %get-tuple-element.127), kind=kOutput, calls=%fused_computation.80.clone.1 | convolution fusion | flops 407373312 | bytes 7344132 | tf_op jit(solution)/shard_map/while/body/eval_jaxpr/sub | solution.py:68
  335.2 4.5 %fusion.83 = bf16[3,512,2,128]{3,1,0,2:T(8,128)(2,1)} fusion(bf16[3,512,2,128]{3,1,0,2:T(8,128)(2,1)} %get-tuple-element.128, s32[]{:T(128)} %get-tuple-element.127, bf16[1536,2,128]{2,0,1:T(8,128)(2,1)S(1)} %get-tuple-element.137, f32[2,512,1536]{2,1,0:T(8,128)} %get-tuple-element.119, f32[2,512]{1,0:T(2,128)S(1)} %get-tuple-element.120), kind=kOutput, calls=%fused_computation.9.clone.1 | convolution fusion | flops 405929984 | bytes 7344640 | tf_op jit(solution)/shard_map/while/body/eval_jaxpr/iqk,kid->qid/dot_general | solution.py:70
  339.7 4.6 %fusion.82 = (f32[2,512]{1,0:T(2,128)S(1)}, f32[2,512,1536]{2,1,0:T(8,128)}) fusion(bf16[1536,2,128]{2,0,1:T(8,128)(2,1)S(1)} %get-tuple-element.136, bf16[3,512,2,128]{3,1,0,2:T(8,128)(2,1)S(1)} %get-tuple-element.135, s32[]{:T(128)} %get-tuple-element.127), kind=kOutput, calls=%fused_computation.80.clone.1 | convolution fusion | flops 407373312 | bytes 7344132 | tf_op jit(solution)/shard_map/while/body/eval_jaxpr/sub | solution.py:68
  344.3 4.5 %fusion.83 = bf16[3,512,2,128]{3,1,0,2:T(8,128)(2,1)} fusion(bf16[3,512,2,128]{3,1,0,2:T(8,128)(2,1)} %get-tuple-element.128, s32[]{:T(128)} %get-tuple-element.127, bf16[1536,2,128]{2,0,1:T(8,128)(2,1)S(1)} %get-tuple-element.137, f32[2,512,1536]{2,1,0:T(8,128)} %get-tuple-element.119, f32[2,512]{1,0:T(2,128)S(1)} %get-tuple-element.120), kind=kOutput, calls=%fused_computation.9.clone.1 | convolution fusion | flops 405929984 | bytes 7344640 | tf_op jit(solution)/shard_map/while/body/eval_jaxpr/iqk,kid->qid/dot_general | solution.py:70
  348.8 6.8 %copy.99 = bf16[1536,2,128]{2,1,0:T(2,128)(2,1)S(1)} copy(bf16[1536,2,128]{2,0,1:T(8,128)(2,1)} %bitcast.40) | data formatting | bytes 1572864 | tf_op jit(solution)/shard_map/reshape | solution.py:74
  355.6 17.3 %all_to_all.53 = bf16[1536,2,128]{2,1,0:T(2,128)(2,1)S(1)} all-to-all(bf16[1536,2,128]{2,1,0:T(2,128)(2,1)S(1)} %copy.99), channel_id=1, replica_groups=mesh['tok'=16,'wid'=8] {'tok'}, dimensions={0} | all-to-all | bytes 1572864 | tf_op jit(solution)/shard_map/all_to_all | solution.py:75
  375.1 41.2 %all-gather.15.cloned.1.call-done = bf16[96,8,4096]{2,1,0:T(8,128)(2,1)} async-done(((bf16[96,8,512]{2,1,0:T(8,128)(2,1)}), bf16[96,8,4096]{2,1,0:T(8,128)(2,1)}) %all-gather.15.cloned.1.call-update) | async-done | bytes 6291472 | tf_op jit(solution)/shard_map/all_gather | solution.py:77
  416.2 9.8 %fusion.38 = bf16[96,8,768]{2,1,0:T(8,128)(2,1)} fusion(bf16[96,8,768]{2,1,0:T(8,128)(2,1)S(1)} %copy-done.1, bf16[96,8,4096]{2,1,0:T(8,128)(2,1)} %all-gather.15.cloned.1.call-done, bf16[4096,768]{1,0:T(8,128)(2,1)} %all-gather.17.cloned.1.call-done), kind=kOutput, calls=%fused_computation.34 | convolution fusion | flops 4833607680 | bytes 14942208 | tf_op jit(solution)/shard_map/dot_general | solution.py:18
  (60 shorter events, 20.1 us)
Async XLA Ops:
  6.5 67.2 %all-gather.11.cloned.1.call-start = ((), (), s32[]{:S(2)}) async-start(), calls=%async_computation.6 | async-start | bytes 6684672 | tf_op jit(solution)/shard_map/all_gather | solution.py:43
  7.3 129.5 %all-gather.9.cloned.1.call-start = ((), (), s32[]{:S(2)}) async-start(), calls=%async_computation.5 | async-start | bytes 6684672 | tf_op jit(solution)/shard_map/all_gather | solution.py:42
  8.0 185.1 %all-gather.7.cloned.1.call-start = ((), (), s32[]{:S(2)}) async-start(), calls=%async_computation.4 | async-start | bytes 10616832 | tf_op jit(solution)/shard_map/all_gather | solution.py:36
  27.5 236.8 %all-gather.13.cloned.1.call-start = ((), (), s32[]{:S(2)}) async-start(), calls=%async_computation.7 | async-start | bytes 6684672 | tf_op jit(solution)/shard_map/all_gather | solution.py:44
  28.1 347.0 %all-gather.17.cloned.1.call-start = ((), (), s32[]{:S(2)}) async-start(), calls=%async_computation.9 | async-start | bytes 6684672 | tf_op jit(solution)/shard_map/all_gather | solution.py:78
  193.1 10.7 %copy-start = (bf16[512,6144]{1,0:T(8,128)(2,1)S(1)}, bf16[512,6144]{1,0:T(8,128)(2,1)}, u32[]{:S(2)}) copy-start(bf16[512,6144]{1,0:T(8,128)(2,1)} %copy.81) | copy-start | bytes 18874372
  193.1 10.7 %copy-start.2 = (bf16[96,8,6144]{2,1,0:T(8,128)(2,1)S(1)}, bf16[96,8,6144]{2,1,0:T(8,128)(2,1)}, u32[]{:S(2)}) copy-start(bf16[96,8,6144]{2,1,0:T(8,128)(2,1)} %all-gather.7.cloned.1.call-done) | copy-start | bytes 28311556
  219.7 58.7 %all-to-all-start = ((bf16[96,32,128]{2,0,1:T(8,128)(2,1)}), bf16[96,32,128]{2,0,1:T(8,128)(2,1)S(1)}, u32[]{:S(2)}, u32[]{:S(2)}) async-start(bf16[96,32,128]{2,0,1:T(8,128)(2,1)} %bitcast.9), calls=%async_computation | async-start | bytes 1572864 | tf_op jit(solution)/shard_map/all_to_all | solution.py:51
  278.3 20.1 %all-to-all-start.2 = ((bf16[96,32,128]{2,0,1:T(8,128)(2,1)}), bf16[96,32,128]{2,0,1:T(8,128)(2,1)S(1)}, u32[]{:S(2)}, u32[]{:S(2)}) async-start(bf16[96,32,128]{2,0,1:T(8,128)(2,1)} %copy.95), calls=%async_computation.2 | async-start | bytes 1572864 | tf_op jit(solution)/shard_map/all_to_all | solution.py:56
  298.5 22.8 %all-to-all-start.1 = ((bf16[16,96,2,128]{3,1,2,0:T(8,128)(2,1)}), bf16[16,96,2,128]{3,1,2,0:T(8,128)(2,1)S(1)}, u32[]{:S(2)}, u32[]{:S(2)}) async-start(bf16[16,96,2,128]{3,1,2,0:T(8,128)(2,1)} %fusion.44), calls=%async_computation.1 | async-start | bytes 1572864 | tf_op jit(solution)/shard_map/all_to_all | solution.py:53
  302.1 114.2 %all-gather.15.cloned.1.call-start = ((), (), s32[]{:S(2)}) async-start(), calls=%async_computation.8 | async-start | bytes 7077888 | tf_op jit(solution)/shard_map/all_gather | solution.py:77
  348.8 67.4 %copy-start.1 = (bf16[96,8,768]{2,1,0:T(8,128)(2,1)S(1)}, bf16[96,8,768]{2,1,0:T(8,128)(2,1)}, u32[]{:S(2)}) copy-start(bf16[96,8,768]{2,1,0:T(8,128)(2,1)} %param.9) | copy-start | bytes 3538948
Sparse Core Ops, SparseCore 0:
  9.5 64.1 all-gather.10
  75.9 60.8 all-gather.8
  138.5 54.5 all-gather.6
  195.1 69.1 all-gather.12
  266.3 73.0 all-gather.16
  375.2 41.0 all-gather.14
